TPU v7x, 256 devices: a whole 4x4x8 slice. The times are simulated.
256 devices in a mesh: dp: 8 (over y_hi, x), seq: 16 (over y_lo, z), segment: 2 (over core).
Axes of the slice: x: 4, y: 4 (y_hi: 2, y_lo: 2; y = y_hi * 2 + y_lo), z: 8, core: 2. Of those that a mesh axis runs over, the one named last changes fastest.
Arguments:
- saved_input: bfloat16 [2, 8, 8192, 256], P('segment', 'dp', 'seq'), may hold values from -6 to 6
- upstream: bfloat16 [8, 8192, 256], P('dp', 'seq'), may hold values from -6 to 6
- clip_lengths: int32 [8, 32], P('dp'), may hold values from 1 to 2048, 8192 in all within a row
- conv_a: bfloat16 [2, 3, 7, 256, 256], P('segment'), may hold values from -0.125 to 0.125
- bias_a: float32 [2, 3, 256], P('segment'), may hold values from -3 to 3
- conv_b: bfloat16 [2, 3, 256, 256], P('segment'), may hold values from -0.375 to 0.375
Outputs:
- section_input_grad: bfloat16 [2, 8, 8192, 256], P('segment', 'dp', 'seq')
- grad_conv_a: float32 [2, 3, 7, 256, 256], P('segment')
- grad_bias_a: float32 [2, 3, 256], P('segment')
- grad_conv_b: float32 [2, 3, 256, 256], P('segment')
Inputs may be any that keep to these rules, and one draw needn't show every extreme that they name: `clip_lengths`: each row's 32 lengths sum to 8192, and the longest is exactly 2048.
All inputs are finite; a program needn't handle non-finite values.
Results may differ from a plain program's by a relative error of at most 0.02.
Values may be sent and summed in bfloat16 or wider, within the bound.
No kernel may reach another device: no remote copies, remote signals or barrier semaphores. Data moves between devices by JAX's collectives and lax.ppermute only.
A program may use at most 128 MiB of HBM per device.

v0:
```python
import jax
import jax.numpy as jnp
from jax import lax
from jax.sharding import PartitionSpec as P

KERNEL = 7
UNITS = 3


def with_halo(cells, sides, width):
    for axis, dim in sides:
        count = lax.axis_size(axis)
        ends = count - 1
        head = lax.slice_in_dim(cells, 0, width, axis=dim)
        tail = lax.slice_in_dim(cells, cells.shape[dim] - width, cells.shape[dim], axis=dim)
        cells = jnp.concatenate(
            [
                lax.ppermute(tail, axis, [(i, (i + 1) % count) for i in range(ends)]),
                cells,
                lax.ppermute(head, axis, [((i + 1) % count, i) for i in range(ends)]),
            ],
            axis=dim,
        )
    return cells


def spread(value, axis, root):
    mine = lax.axis_index(axis) == root
    return lax.psum(jnp.where(mine, value, jnp.zeros_like(value)), axis)


def elu_act(value):
    return jnp.where(value > 0, value, jnp.expm1(jnp.minimum(value, 0.0)))


def elu_slope(value):
    return jnp.where(value > 0, 1.0, jnp.exp(jnp.minimum(value, 0.0)))


def spread_acts(active, reach):
    return with_halo(active, (("seq", 0),), reach)


def spread_grads(gate, reach):
    return with_halo(gate, (("seq", 0),), reach)


def shards(saved_input, upstream, clip_lengths, conv_a, bias_a, conv_b):
    stream = saved_input[0, 0]
    lengths = clip_lengths[0]
    weights_a = conv_a[0]
    biases_a = bias_a[0]
    weights_b = conv_b[0]
    frames = stream.shape[0]
    channels = stream.shape[1]
    inner = weights_a.shape[3]
    half = KERNEL // 2
    furthest = half * 3 ** (UNITS - 1)
    offset = lax.axis_index("seq") * frames
    is_decoder = lax.axis_index("segment") == 1
    clip_ends = jnp.cumsum(lengths)
    places = offset - furthest + jnp.arange(frames + 2 * furthest, dtype=jnp.int32)
    clip_of = jnp.sum((places[:, None] >= clip_ends[None, :]).astype(jnp.int32), axis=1)
    own_clip = clip_of[furthest : furthest + frames]

    def linked(shift_by):
        return (clip_of[furthest + shift_by : furthest + shift_by + frames] == own_clip)[:, None]

    stored = []
    for unit_idx in range(UNITS):
        dilation = 3**unit_idx
        reach = half * dilation
        active = elu_act(stream.astype(jnp.float32)).astype(jnp.bfloat16)
        padded = spread_acts(active, reach)
        tap_rows = jnp.concatenate(
            [
                jnp.where(
                    linked((tap_no - half) * dilation),
                    padded[
                        reach
                        + (tap_no - half) * dilation : reach
                        + (tap_no - half) * dilation
                        + frames
                    ],
                    jnp.zeros((), jnp.bfloat16),
                )
                for tap_no in range(KERNEL)
            ],
            axis=1,
        )
        pre_act = biases_a[unit_idx][None, :] + jnp.dot(
            tap_rows,
            weights_a[unit_idx].reshape(KERNEL * channels, inner),
            preferred_element_type=jnp.float32,
        )
        squashed = elu_act(pre_act).astype(jnp.bfloat16)
        next_stream = (
            stream.astype(jnp.float32)
            + jnp.dot(squashed, weights_b[unit_idx], preferred_element_type=jnp.float32)
        ).astype(jnp.bfloat16)
        stored.append((stream, tap_rows, pre_act, squashed))
        stream = next_stream

    def unit_back(unit_idx, grad_y):
        dilation = 3**unit_idx
        reach = half * dilation
        stream_in, tap_rows, pre_act, squashed = stored[unit_idx]
        grad_b = lax.dot_general(
            grad_y,
            weights_b[unit_idx],
            (((1,), (1,)), ((), ())),
            preferred_element_type=jnp.float32,
        )
        gate = (grad_b * elu_slope(pre_act)).astype(jnp.bfloat16)
        gate_padded = spread_grads(gate, reach)
        back_rows = jnp.concatenate(
            [
                jnp.where(
                    linked(-(tap_no - half) * dilation),
                    gate_padded[
                        reach
                        - (tap_no - half) * dilation : reach
                        - (tap_no - half) * dilation
                        + frames
                    ],
                    jnp.zeros((), jnp.bfloat16),
                )
                for tap_no in range(KERNEL)
            ],
            axis=1,
        )
        turned = jnp.transpose(weights_a[unit_idx], (0, 2, 1)).reshape(KERNEL * inner, channels)
        back = jnp.dot(back_rows, turned, preferred_element_type=jnp.float32)
        grad_next = (
            grad_y.astype(jnp.float32) + back * elu_slope(stream_in.astype(jnp.float32))
        ).astype(jnp.bfloat16)
        return (gate, grad_next)

    first_gates = [None] * UNITS
    first_grads = [None] * (UNITS + 1)
    grad_y = upstream[0]
    first_grads[UNITS] = grad_y
    for unit_idx in reversed(range(UNITS)):
        gate, grad_y = unit_back(unit_idx, grad_y)
        first_gates[unit_idx] = gate
        first_grads[unit_idx] = grad_y
    latent = spread(grad_y, "segment", 1)
    grads_a = [None] * UNITS
    grads_bias = [None] * UNITS
    grads_b = [None] * UNITS
    contract = (((0,), (0,)), ((), ()))
    grad_y = latent
    for unit_idx in reversed(range(UNITS)):
        stream_in, tap_rows, pre_act, squashed = stored[unit_idx]
        gate_two, grad_next = unit_back(unit_idx, grad_y)
        gate = jnp.where(is_decoder, first_gates[unit_idx], gate_two)
        grad_out = jnp.where(is_decoder, first_grads[unit_idx + 1], grad_y)
        unit_b = lax.dot_general(squashed, grad_out, contract, preferred_element_type=jnp.float32)
        unit_bias = jnp.sum(gate.astype(jnp.float32), axis=0)
        unit_a = lax.dot_general(
            tap_rows, gate, contract, preferred_element_type=jnp.float32
        ).reshape(KERNEL, channels, inner)
        grads_a[unit_idx] = unit_a
        grads_bias[unit_idx] = unit_bias
        grads_b[unit_idx] = unit_b
        grad_y = grad_next
    section_grad = jnp.where(is_decoder, first_grads[0], grad_y)
    total_a = jnp.stack(grads_a)
    total_bias = jnp.stack(grads_bias)
    total_b = jnp.stack(grads_b)
    total_a, total_bias, total_b = lax.psum((total_a, total_bias, total_b), ("dp", "seq"))
    return (section_grad[None, None], total_a[None], total_bias[None], total_b[None])


def solution(mesh):
    placed = (
        P("segment", "dp", "seq", None),
        P("dp", "seq", None),
        P("dp", None),
        P("segment", None, None, None, None),
        P("segment", None, None),
        P("segment", None, None, None),
    )
    return jax.shard_map(
        shards,
        mesh=mesh,
        in_specs=placed,
        out_specs=(
            P("segment", "dp", "seq", None),
            P("segment", None, None, None, None),
            P("segment", None, None),
            P("segment", None, None, None),
        ),
        check_vma=False,
    )
```

profile of v0, /device:TPU:32, one launch (start us, length us, event | category | flops | bytes accessed | tf_op | source)
XLA Modules:
  0.0 530.8 jit_solution(7893162154168476364)
XLA Ops:
  7.2 1.2 fusion.32
  8.4 3.7 collective-permute-start.1
  12.1 2.1 collective-permute-start
  14.3 0.7 copy.19
  15.6 3.7 slice_bitcast_fusion.2
  21.9 3.8 collective-permute-start.2
  25.7 2.0 collective-permute-start.3
  28.3 4.1 collective-permute-done.3
  34.5 3.9 collective-permute-start.4
  38.5 1.9 collective-permute-start.5
  40.9 4.3 collective-permute-done.5
  47.8 1.9 collective-permute-start.6
  49.7 2.2 copy.20
  52.0 4.1 collective-permute-start.7
  56.1 0.8 fusion.128
  56.8 0.8 fusion.125
  57.6 0.8 fusion.165
  60.0 1.3 fusion.17
  61.3 1.9 collective-permute-start.8
  63.3 2.2 copy.21
  65.5 4.1 collective-permute-start.9
  70.1 1.1 collective-permute-done.9
  72.7 1.3 fusion.18
  74.6 1.9 collective-permute-start.10
  76.5 1.4 copy.22
  77.9 4.4 collective-permute-start.11
  82.3 0.8 fusion.56
  83.1 0.8 fusion.53
  83.9 0.8 fusion.157
  85.3 1.5 broadcast_select_fusion.3
  86.9 37.4 %all-reduce.4.cloned.1.call-done = bf16[512,256]{1,0:T(8,128)(2,1)} async-done(((bf16[512,256]{1,0:T(8,128)(2,1)}), bf16[512,256]{1,0:T(8,128)(2,1)}) %all-reduce.4.cloned.1.call-update) | async-done | bytes 262160 | tf_op jit(solution)/shard_map/psum | solution.py:29
  124.3 2.1 convert_reduce_fusion
  126.4 2.3 fusion.203
  128.7 3.5 collective-permute-start.13
  132.2 2.4 collective-permute-start.12
  135.0 2.8 collective-permute-done.12
  141.3 2.4 collective-permute-start.14
  144.1 3.9 collective-permute-start.15
  148.5 1.3 collective-permute-done.15
  152.8 2.8 maximum_bitcast_fusion
  155.6 0.9 maximum_bitcast_fusion.1
  157.2 1.9 collective-permute-start.16
  159.1 349.1 %psum.30 = f32[1,3,256]{2,0,1:T(1,128)} all-reduce(f32[1,3,256]{2,0,1:T(1,128)S(1)} %broadcast_in_dim.397), channel_id=1, replica_groups=mesh['dp'=8,'seq'=16,'segment'=2] {'dp','seq'}, use_global_device_ids=true, to_apply=%region_7.8 | all-reduce | flops 768 | bytes 6144 | tf_op jit(solution)/shard_map/psum | solution.py:171
  508.2 2.0 collective-permute-start.17
  510.8 4.8 collective-permute-done.17
  516.0 1.4 fusion.23
  517.4 5.6 %copy.80 = f32[1,3,7,256,256]{4,3,2,1,0:T(8,128)} copy(f32[1,3,7,256,256]{4,3,2,1,0:T(8,128)} %get-tuple-element.60) | data formatting | bytes 11010048
  523.0 0.9 copy.81
  (259 shorter events, 22.0 us)
Async XLA Ops:
  7.2 117.1 %all-reduce.4.cloned.1.call-start = ((), (), s32[]{:S(2)}) async-start(), calls=%async_computation | async-start | bytes 524288 | tf_op jit(solution)/shard_map/psum | solution.py:29
  8.4 11.6 %collective-permute-start.1 = (bf16[3,256]{1,0:T(4,128)(2,1)S(1)}, bf16[3,256]{1,0:T(4,128)(2,1)S(1)}, u32[]{:S(2)}, u32[]{:S(2)}) collective-permute-start(bf16[3,256]{1,0:T(4,128)(2,1)S(1)} %get-tuple-element.28), channel_id=1, source_target_pairs={{2,0},{4,2},{6,4},{8,6},{10,8},{12,10},{14,12},{16,14},{18,16},{20... | collective-permute-start | bytes 4616 | tf_op jit(solution)/shard_map/ppermute | solution.py:20
  12.1 7.2 %collective-permute-start = (bf16[3,256]{1,0:T(4,128)(2,1)S(1)}, bf16[3,256]{1,0:T(4,128)(2,1)S(1)}, u32[]{:S(2)}, u32[]{:S(2)}) collective-permute-start(bf16[3,256]{1,0:T(4,128)(2,1)S(1)} %get-tuple-element.29), channel_id=1, source_target_pairs={{0,2},{2,4},{4,6},{6,8},{8,10},{10,12},{12,14},{14,16},{16,18},{18... | collective-permute-start | bytes 4616 | tf_op jit(solution)/shard_map/ppermute | solution.py:18
  15.4 12.7 %copy-start.29 = (pred[512]{0:T(512)(128)(4,1)}, pred[512]{0:T(512)(128)(4,1)S(1)}, u32[]{:S(2)}) copy-start(pred[512]{0:T(512)(128)(4,1)S(1)} %get-tuple-element.42) | copy-start | bytes 1540
  15.4 25.0 %copy-start.52 = (pred[512]{0:T(512)(128)(4,1)}, pred[512]{0:T(512)(128)(4,1)S(1)}, u32[]{:S(2)}) copy-start(pred[512]{0:T(512)(128)(4,1)S(1)} %get-tuple-element.43) | copy-start | bytes 1540
  15.4 30.0 %copy-start.55 = (pred[512]{0:T(512)(128)(4,1)}, pred[512]{0:T(512)(128)(4,1)S(1)}, u32[]{:S(2)}) copy-start(pred[512]{0:T(512)(128)(4,1)S(1)} %get-tuple-element.39) | copy-start | bytes 1540
  15.5 12.4 %copy-start.35 = (pred[512]{0:T(512)(128)(4,1)}, pred[512]{0:T(512)(128)(4,1)S(1)}, u32[]{:S(2)}) copy-start(pred[512]{0:T(512)(128)(4,1)S(1)} %get-tuple-element.34) | copy-start | bytes 1540
  15.5 16.9 %copy-start.22 = (pred[512]{0:T(512)(128)(4,1)}, pred[512]{0:T(512)(128)(4,1)S(1)}, u32[]{:S(2)}) copy-start(pred[512]{0:T(512)(128)(4,1)S(1)} %get-tuple-element.36) | copy-start | bytes 1540
  15.5 17.0 %copy-start.38 = (pred[512]{0:T(512)(128)(4,1)}, pred[512]{0:T(512)(128)(4,1)S(1)}, u32[]{:S(2)}) copy-start(pred[512]{0:T(512)(128)(4,1)S(1)} %get-tuple-element.33) | copy-start | bytes 1540
  15.5 25.0 %copy-start.41 = (pred[512]{0:T(512)(128)(4,1)}, pred[512]{0:T(512)(128)(4,1)S(1)}, u32[]{:S(2)}) copy-start(pred[512]{0:T(512)(128)(4,1)S(1)} %get-tuple-element.31) | copy-start | bytes 1540
  15.5 25.2 %copy-start.24 = (pred[512]{0:T(512)(128)(4,1)}, pred[512]{0:T(512)(128)(4,1)S(1)}, u32[]{:S(2)}) copy-start(pred[512]{0:T(512)(128)(4,1)S(1)} %get-tuple-element.35) | copy-start | bytes 1540
  15.6 29.7 %copy-start.27 = (pred[512]{0:T(512)(128)(4,1)}, pred[512]{0:T(512)(128)(4,1)S(1)}, u32[]{:S(2)}) copy-start(pred[512]{0:T(512)(128)(4,1)S(1)} %get-tuple-element.32) | copy-start | bytes 1540
  15.6 30.0 %copy-start.44 = (pred[512]{0:T(512)(128)(4,1)}, pred[512]{0:T(512)(128)(4,1)S(1)}, u32[]{:S(2)}) copy-start(pred[512]{0:T(512)(128)(4,1)S(1)} %get-tuple-element.30) | copy-start | bytes 1540
  21.9 12.2 %copy-start.12 = (f32[512,256]{1,0:T(8,128)}, f32[512,256]{1,0:T(8,128)S(1)}, u32[]{:S(2)}) copy-start(f32[512,256]{1,0:T(8,128)S(1)} %get-tuple-element.48) | copy-start | bytes 1572868
  21.9 5.9 %collective-permute-start.2 = (bf16[9,256]{1,0:T(8,128)(2,1)S(1)}, bf16[9,256]{1,0:T(8,128)(2,1)S(1)}, u32[]{:S(2)}, u32[]{:S(2)}) collective-permute-start(bf16[9,256]{1,0:T(8,128)(2,1)S(1)} %get-tuple-element.27), channel_id=1, source_target_pairs={{0,2},{2,4},{4,6},{6,8},{8,10},{10,12},{12,14},{14,16},{16,18},{18... | collective-permute-start | bytes 13832 | tf_op jit(solution)/shard_map/ppermute | solution.py:18
  25.7 6.7 %collective-permute-start.3 = (bf16[9,256]{1,0:T(8,128)(2,1)S(1)}, bf16[9,256]{1,0:T(8,128)(2,1)S(1)}, u32[]{:S(2)}, u32[]{:S(2)}) collective-permute-start(bf16[9,256]{1,0:T(8,128)(2,1)S(1)} %get-tuple-element.26), channel_id=1, source_target_pairs={{2,0},{4,2},{6,4},{8,6},{10,8},{12,10},{14,12},{16,14},{18,16},{20... | collective-permute-start | bytes 13832 | tf_op jit(solution)/shard_map/ppermute | solution.py:20
  34.5 24.4 %copy-start.18 = (f32[512,256]{1,0:T(8,128)}, f32[512,256]{1,0:T(8,128)S(1)}, u32[]{:S(2)}) copy-start(f32[512,256]{1,0:T(8,128)S(1)} %get-tuple-element.50) | copy-start | bytes 1572868
  34.5 5.9 %collective-permute-start.4 = (bf16[27,256]{1,0:T(8,128)(2,1)S(1)}, bf16[27,256]{1,0:T(8,128)(2,1)S(1)}, u32[]{:S(2)}, u32[]{:S(2)}) collective-permute-start(bf16[27,256]{1,0:T(8,128)(2,1)S(1)} %get-tuple-element.25), channel_id=1, source_target_pairs={{0,2},{2,4},{4,6},{6,8},{8,10},{10,12},{12,14},{14,16},{16,18},{18... | collective-permute-start | bytes 41480 | tf_op jit(solution)/shard_map/ppermute | solution.py:18
  38.5 6.7 %collective-permute-start.5 = (bf16[27,256]{1,0:T(8,128)(2,1)S(1)}, bf16[27,256]{1,0:T(8,128)(2,1)S(1)}, u32[]{:S(2)}, u32[]{:S(2)}) collective-permute-start(bf16[27,256]{1,0:T(8,128)(2,1)S(1)} %get-tuple-element.24), channel_id=1, source_target_pairs={{2,0},{4,2},{6,4},{8,6},{10,8},{12,10},{14,12},{16,14},{18,16},{20... | collective-permute-start | bytes 41480 | tf_op jit(solution)/shard_map/ppermute | solution.py:20
  47.8 8.2 %collective-permute-start.6 = (bf16[27,256]{1,0:T(8,128)(2,1)}, bf16[27,256]{1,0:T(8,128)(2,1)S(1)}, u32[]{:S(2)}, u32[]{:S(2)}) collective-permute-start(bf16[27,256]{1,0:T(8,128)(2,1)} %get-tuple-element.23), channel_id=1, source_target_pairs={{2,0},{4,2},{6,4},{8,6},{10,8},{12,10},{14,12},{16,14},{18,16},{20... | collective-permute-start | bytes 41480 | tf_op jit(solution)/shard_map/ppermute | solution.py:20
  52.0 6.5 %collective-permute-start.7 = (bf16[27,256]{1,0:T(8,128)(2,1)}, bf16[27,256]{1,0:T(8,128)(2,1)S(1)}, u32[]{:S(2)}, u32[]{:S(2)}) collective-permute-start(bf16[27,256]{1,0:T(8,128)(2,1)} %get-tuple-element.22), channel_id=1, source_target_pairs={{0,2},{2,4},{4,6},{6,8},{8,10},{10,12},{12,14},{14,16},{16,18},{18... | collective-permute-start | bytes 41480 | tf_op jit(solution)/shard_map/ppermute | solution.py:18
  60.0 9.6 %copy-start.28 = (pred[512]{0:T(512)(128)(4,1)S(1)}, pred[512]{0:T(512)(128)(4,1)}, u32[]{:S(2)}) copy-start(pred[512]{0:T(512)(128)(4,1)} %copy-done.27) | copy-start | bytes 1540
  60.0 9.8 %copy-start.39 = (pred[512]{0:T(512)(128)(4,1)S(1)}, pred[512]{0:T(512)(128)(4,1)}, u32[]{:S(2)}) copy-start(pred[512]{0:T(512)(128)(4,1)} %copy-done.38) | copy-start | bytes 1540
  60.0 9.9 %copy-start.23 = (pred[512]{0:T(512)(128)(4,1)S(1)}, pred[512]{0:T(512)(128)(4,1)}, u32[]{:S(2)}) copy-start(pred[512]{0:T(512)(128)(4,1)} %copy-done.22) | copy-start | bytes 1540
  61.3 8.3 %collective-permute-start.8 = (bf16[9,256]{1,0:T(8,128)(2,1)S(1)}, bf16[9,256]{1,0:T(8,128)(2,1)S(1)}, u32[]{:S(2)}, u32[]{:S(2)}) collective-permute-start(bf16[9,256]{1,0:T(8,128)(2,1)S(1)} %get-tuple-element.21), channel_id=1, source_target_pairs={{2,0},{4,2},{6,4},{8,6},{10,8},{12,10},{14,12},{16,14},{18,16},{20... | collective-permute-start | bytes 13832 | tf_op jit(solution)/shard_map/ppermute | solution.py:20
  63.3 8.0 %copy-start.30 = (pred[512]{0:T(512)(128)(4,1)S(1)}, pred[512]{0:T(512)(128)(4,1)}, u32[]{:S(2)}) copy-start(pred[512]{0:T(512)(128)(4,1)} %copy-done.29) | copy-start | bytes 1540
  63.3 8.1 %copy-start.36 = (pred[512]{0:T(512)(128)(4,1)S(1)}, pred[512]{0:T(512)(128)(4,1)}, u32[]{:S(2)}) copy-start(pred[512]{0:T(512)(128)(4,1)} %copy-done.35) | copy-start | bytes 1540
  65.5 5.7 %collective-permute-start.9 = (bf16[9,256]{1,0:T(8,128)(2,1)S(1)}, bf16[9,256]{1,0:T(8,128)(2,1)S(1)}, u32[]{:S(2)}, u32[]{:S(2)}) collective-permute-start(bf16[9,256]{1,0:T(8,128)(2,1)S(1)} %get-tuple-element.20), channel_id=1, source_target_pairs={{0,2},{2,4},{4,6},{6,8},{8,10},{10,12},{12,14},{14,16},{16,18},{18... | collective-permute-start | bytes 13832 | tf_op jit(solution)/shard_map/ppermute | solution.py:18
  74.6 7.7 %collective-permute-start.10 = (bf16[3,256]{1,0:T(4,128)(2,1)}, bf16[3,256]{1,0:T(4,128)(2,1)}, u32[]{:S(2)}, u32[]{:S(2)}) collective-permute-start(bf16[3,256]{1,0:T(4,128)(2,1)} %get-tuple-element.19), channel_id=1, source_target_pairs={{2,0},{4,2},{6,4},{8,6},{10,8},{12,10},{14,12},{16,14},{18,16},{20... | collective-permute-start | bytes 4616 | tf_op jit(solution)/shard_map/ppermute | solution.py:20
  77.9 6.9 %collective-permute-start.11 = (bf16[3,256]{1,0:T(4,128)(2,1)}, bf16[3,256]{1,0:T(4,128)(2,1)S(1)}, u32[]{:S(2)}, u32[]{:S(2)}) collective-permute-start(bf16[3,256]{1,0:T(4,128)(2,1)} %get-tuple-element.18), channel_id=1, source_target_pairs={{0,2},{2,4},{4,6},{6,8},{8,10},{10,12},{12,14},{14,16},{16,18},{18... | collective-permute-start | bytes 4616 | tf_op jit(solution)/shard_map/ppermute | solution.py:18
  86.8 430.6 %all-reduce.6.cloned.1.call-start = ((), (), s32[]{:S(2)}) async-start(), calls=%async_computation.1 | async-start | bytes 12582912 | tf_op jit(solution)/shard_map/psum | solution.py:171
  126.4 8.2 %copy-start.61 = (bf16[1,512,256]{2,1,0:T(8,128)(2,1)S(1)}, bf16[1,512,256]{2,1,0:T(8,128)(2,1)}, u32[]{:S(2)}) copy-start(bf16[1,512,256]{2,1,0:T(8,128)(2,1)} %param.7) | copy-start | bytes 786436
  126.4 8.2 %copy-start.62 = (bf16[512,256]{1,0:T(8,128)(2,1)S(1)}, bf16[512,256]{1,0:T(8,128)(2,1)}, u32[]{:S(2)}) copy-start(bf16[512,256]{1,0:T(8,128)(2,1)} %all-reduce.4.cloned.1.call-done) | copy-start | bytes 786436
  126.4 8.2 %copy-start.67 = (f32[512,256]{1,0:T(8,128)S(1)}, f32[512,256]{1,0:T(8,128)}, u32[]{:S(2)}) copy-start(f32[512,256]{1,0:T(8,128)} %copy-done.66) | copy-start | bytes 1572868
  126.4 11.4 %copy-start.45 = (pred[512]{0:T(512)(128)(4,1)S(1)}, pred[512]{0:T(512)(128)(4,1)}, u32[]{:S(2)}) copy-start(pred[512]{0:T(512)(128)(4,1)} %copy-done.44) | copy-start | bytes 1540
  128.7 9.3 %copy-start.56 = (pred[512]{0:T(512)(128)(4,1)S(1)}, pred[512]{0:T(512)(128)(4,1)}, u32[]{:S(2)}) copy-start(pred[512]{0:T(512)(128)(4,1)} %copy-done.55) | copy-start | bytes 1540
  128.7 9.6 %collective-permute-start.13 = (bf16[27,256]{1,0:T(8,128)(2,1)S(1)}, bf16[27,256]{1,0:T(8,128)(2,1)S(1)}, u32[]{:S(2)}, u32[]{:S(2)}) collective-permute-start(bf16[27,256]{1,0:T(8,128)(2,1)S(1)} %get-tuple-element.16), channel_id=1, source_target_pairs={{0,2},{2,4},{4,6},{6,8},{8,10},{10,12},{12,14},{14,16},{16,18},{18... | collective-permute-start | bytes 41480 | tf_op jit(solution)/shard_map/ppermute | solution.py:18
  132.2 5.6 %collective-permute-start.12 = (bf16[27,256]{1,0:T(8,128)(2,1)S(1)}, bf16[27,256]{1,0:T(8,128)(2,1)S(1)}, u32[]{:S(2)}, u32[]{:S(2)}) collective-permute-start(bf16[27,256]{1,0:T(8,128)(2,1)S(1)} %get-tuple-element.17), channel_id=1, source_target_pairs={{2,0},{4,2},{6,4},{8,6},{10,8},{12,10},{14,12},{16,14},{18,16},{20... | collective-permute-start | bytes 41480 | tf_op jit(solution)/shard_map/ppermute | solution.py:20
  141.3 8.7 %copy-start.37 = (pred[512]{0:T(512)(128)(4,1)S(1)}, pred[512]{0:T(512)(128)(4,1)}, u32[]{:S(2)}) copy-start(pred[512]{0:T(512)(128)(4,1)} %copy-done.35) | copy-start | bytes 1540
  141.3 6.7 %collective-permute-start.14 = (bf16[9,256]{1,0:T(8,128)(2,1)S(1)}, bf16[9,256]{1,0:T(8,128)(2,1)S(1)}, u32[]{:S(2)}, u32[]{:S(2)}) collective-permute-start(bf16[9,256]{1,0:T(8,128)(2,1)S(1)} %get-tuple-element.15), channel_id=1, source_target_pairs={{2,0},{4,2},{6,4},{8,6},{10,8},{12,10},{14,12},{16,14},{18,16},{20... | collective-permute-start | bytes 13832 | tf_op jit(solution)/shard_map/ppermute | solution.py:20
  144.1 5.7 %collective-permute-start.15 = (bf16[9,256]{1,0:T(8,128)(2,1)S(1)}, bf16[9,256]{1,0:T(8,128)(2,1)S(1)}, u32[]{:S(2)}, u32[]{:S(2)}) collective-permute-start(bf16[9,256]{1,0:T(8,128)(2,1)S(1)} %get-tuple-element.14), channel_id=1, source_target_pairs={{0,2},{2,4},{4,6},{6,8},{8,10},{10,12},{12,14},{14,16},{16,18},{18... | collective-permute-start | bytes 13832 | tf_op jit(solution)/shard_map/ppermute | solution.py:18
  156.5 353.9 %copy-start.34 = (pred[512]{0:T(512)(128)(4,1)S(1)}, pred[512]{0:T(512)(128)(4,1)}, u32[]{:S(2)}) copy-start(pred[512]{0:T(512)(128)(4,1)} %copy-done.33) | copy-start | bytes 1540
  156.5 354.1 %copy-start.32 = (pred[512]{0:T(512)(128)(4,1)S(1)}, pred[512]{0:T(512)(128)(4,1)}, u32[]{:S(2)}) copy-start(pred[512]{0:T(512)(128)(4,1)} %copy-done.31) | copy-start | bytes 1540
  156.5 359.0 %copy-start.51 = (pred[512]{0:T(512)(128)(4,1)S(1)}, pred[512]{0:T(512)(128)(4,1)}, u32[]{:S(2)}) copy-start(pred[512]{0:T(512)(128)(4,1)} %copy-done.49) | copy-start | bytes 1540
  156.6 359.1 %copy-start.48 = (pred[512]{0:T(512)(128)(4,1)S(1)}, pred[512]{0:T(512)(128)(4,1)}, u32[]{:S(2)}) copy-start(pred[512]{0:T(512)(128)(4,1)} %copy-done.46) | copy-start | bytes 1540
  157.2 353.1 %collective-permute-start.16 = (bf16[3,256]{1,0:T(4,128)(2,1)S(1)}, bf16[3,256]{1,0:T(4,128)(2,1)S(1)}, u32[]{:S(2)}, u32[]{:S(2)}) collective-permute-start(bf16[3,256]{1,0:T(4,128)(2,1)S(1)} %get-tuple-element.13), channel_id=1, source_target_pairs={{2,0},{4,2},{6,4},{8,6},{10,8},{12,10},{14,12},{16,14},{18,16},{20... | collective-permute-start | bytes 4616 | tf_op jit(solution)/shard_map/ppermute | solution.py:20
  508.2 7.7 %copy-start.74 = (bf16[512,256]{1,0:T(8,128)(2,1)S(1)}, bf16[512,256]{1,0:T(8,128)(2,1)}, u32[]{:S(2)}) copy-start(bf16[512,256]{1,0:T(8,128)(2,1)} %get-tuple-element.52) | copy-start | bytes 786436
  508.2 7.3 %collective-permute-start.17 = (bf16[3,256]{1,0:T(4,128)(2,1)S(1)}, bf16[3,256]{1,0:T(4,128)(2,1)S(1)}, u32[]{:S(2)}, u32[]{:S(2)}) collective-permute-start(bf16[3,256]{1,0:T(4,128)(2,1)S(1)} %get-tuple-element.12), channel_id=1, source_target_pairs={{0,2},{2,4},{4,6},{6,8},{8,10},{10,12},{12,14},{14,16},{16,18},{18... | collective-permute-start | bytes 4616 | tf_op jit(solution)/shard_map/ppermute | solution.py:18
  (47 other events, 205.2 us)
Sparse Core Ops, SparseCore 0:
  86.9 37.3 all-reduce.3
  156.7 249.6 all-reduce.5
where the time goes:
time: 532 us; the launch traced here: 531 us
  blocking collectives  349 us (66%)
  waiting for transfers between devices  55.9 us (11%)
  starting transfers between devices  51.9 us (10%)
  local copies, waits for them, and re-layouts  22.6 us (4%)
  matrix products  18.8 us (4%)
  other arithmetic  16.8 us (3%)
  between operations  15.8 us (3%)
    psum x1, blocking collectives, shards(): lax.psum((total_a, total_bias, total_b), ('dp', 'seq'))  349 us
    psum x1, waiting for transfers between devices, spread(): return lax.psum(jnp.where(mine, value, jnp.zeros_like(value)), axis)  37.4 us
    ppermute x9, starting transfers between devices, with_halo(): lax.ppermute(tail, axis, [(i, (i + 1) % count) for i in range(ends)])  31.7 us
    ppermute x9, starting transfers between devices, with_halo(): lax.ppermute(head, axis, [((i + 1) % count, i) for i in range(ends)])  20.1 us
    ppermute x9, waiting for transfers between devices, with_halo(): lax.ppermute(head, axis, [((i + 1) % count, i) for i in range(ends)])  11.2 us
    unnamed x160, local copies, waits for them, and re-layouts  11 us
  transfers between devices with their start and end apart: 20, of which 7 were waited for; matrix products, arithmetic and copies ran while one was open for 4% of the time, Pallas kernels for 0%

commit v1 on v0

--- a/solution.py
+++ b/solution.py
@@ -26,7 +26,7 @@
 
 def spread(value, axis, root):
     mine = lax.axis_index(axis) == root
-    return lax.psum(jnp.where(mine, value, jnp.zeros_like(value)), axis)
+    return jnp.sum(jax.lax.all_gather(jnp.where(mine, value, jnp.zeros_like(value)), axis), axis=0)
 
 
 def elu_act(value):

time: 532 us -> 505 us (0.949)
  waiting for transfers between devices: 55.9 us -> 17.3 us
  blocking collectives: 349 us -> 357 us
    psum x1 -> x0, waiting for transfers between devices: 37.4 us -> none  [spread(): return lax.psum(jnp.where(mine, value, jnp.zeros_like(value)), axis)]
    psum x1, blocking collectives: 349 us -> 355 us  [shards(): lax.psum((total_a, total_bias, total_b), ('dp', 'seq'))]
  transfers between devices with their start and end apart: 20 -> 19, of which waited for: 7 -> 6; matrix products, arithmetic and copies ran while one was open for 4% -> 4% of each run, Pallas kernels for 0% -> 0%
where the time goes in v1:
time: 505 us; the launch traced here: 504 us
  blocking collectives  357 us (71%)
  starting transfers between devices  54.8 us (11%)
  local copies, waits for them, and re-layouts  22.6 us (4%)
  matrix products  18.6 us (4%)
  other arithmetic  17.6 us (3%)
  waiting for transfers between devices  17.3 us (3%)
  between operations  15.8 us (3%)
    psum x1, blocking collectives, shards(): lax.psum((total_a, total_bias, total_b), ('dp', 'seq'))  355 us
    ppermute x9, starting transfers between devices, with_halo(): lax.ppermute(tail, axis, [(i, (i + 1) % count) for i in range(ends)])  35.6 us
    ppermute x9, starting transfers between devices, with_halo(): lax.ppermute(head, axis, [((i + 1) % count, i) for i in range(ends)])  19.2 us
    unnamed x160, local copies, waits for them, and re-layouts  11 us
    unnamed x46, other arithmetic  10.2 us
  transfers between devices with their start and end apart: 19, of which 6 were waited for; matrix products, arithmetic and copies ran while one was open for 4% of the time, Pallas kernels for 0%

profile of v1, /device:TPU:32, one launch (start us, length us, event | category | flops | bytes accessed | tf_op | source)
XLA Modules:
  0.0 504.0 jit_solution(15003480549889614042)
XLA Ops:
  7.2 1.2 fusion.32
  8.4 3.7 collective-permute-start.1
  12.1 2.1 collective-permute-start
  15.6 3.7 slice_bitcast_fusion.2
  21.9 3.8 collective-permute-start.2
  25.8 2.0 collective-permute-start.3
  28.3 4.1 collective-permute-done.3
  34.6 3.9 collective-permute-start.4
  38.5 1.9 collective-permute-start.5
  40.9 4.3 collective-permute-done.5
  47.8 1.9 collective-permute-start.6
  49.8 2.2 copy.20
  52.0 4.1 collective-permute-start.7
  56.1 0.8 fusion.128
  56.8 0.7 fusion.125
  57.6 0.8 fusion.165
  60.0 1.3 fusion.17
  61.3 1.9 collective-permute-start.8
  63.2 2.2 copy.21
  65.5 4.1 collective-permute-start.9
  70.0 1.1 collective-permute-done.9
  72.7 1.3 fusion.18
  74.6 1.9 collective-permute-start.10
  76.5 1.4 copy.22
  77.9 4.4 collective-permute-start.11
  82.3 0.8 fusion.56
  83.1 0.8 fusion.53
  83.9 0.8 fusion.157
  85.2 1.4 broadcast_select_fusion.3
  86.6 2.2 all-gather
  88.8 0.8 reduce_sum.49
  89.6 2.1 convert_reduce_fusion
  91.7 2.3 fusion.203
  94.0 1.9 collective-permute-start.12
  96.4 5.3 %collective-permute-start.13 = (bf16[27,256]{1,0:T(8,128)(2,1)S(1)}, bf16[27,256]{1,0:T(8,128)(2,1)S(1)}, u32[]{:S(2)}, u32[]{:S(2)}) collective-permute-start(bf16[27,256]{1,0:T(8,128)(2,1)S(1)} %get-tuple-element.16), channel_id=1, source_target_pairs={{0,2},{2,4},{4,6},{6,8},{8,10},{10,12},{12,14},{14,16},{16,18},{18... | collective-permute-start | bytes 41480 | tf_op jit(solution)/shard_map/ppermute | solution.py:18
  102.2 0.9 collective-permute-done.13
  106.1 1.9 collective-permute-start.14
  108.5 5.5 %collective-permute-start.15 = (bf16[9,256]{1,0:T(8,128)(2,1)S(1)}, bf16[9,256]{1,0:T(8,128)(2,1)S(1)}, u32[]{:S(2)}, u32[]{:S(2)}) collective-permute-start(bf16[9,256]{1,0:T(8,128)(2,1)S(1)} %get-tuple-element.14), channel_id=1, source_target_pairs={{0,2},{2,4},{4,6},{6,8},{8,10},{10,12},{12,14},{14,16},{16,18},{18... | collective-permute-start | bytes 13832 | tf_op jit(solution)/shard_map/ppermute | solution.py:18
  114.5 0.9 collective-permute-done.15
  118.4 2.8 maximum_bitcast_fusion
  121.2 0.9 maximum_bitcast_fusion.1
  122.8 1.9 collective-permute-start.16
  124.7 355.1 %psum.22 = f32[1,3,256]{2,0,1:T(1,128)} all-reduce(f32[1,3,256]{2,0,1:T(1,128)S(1)} %broadcast_in_dim.397), channel_id=1, replica_groups=mesh['dp'=8,'seq'=16,'segment'=2] {'dp','seq'}, use_global_device_ids=true, to_apply=%region_7.8 | all-reduce | flops 768 | bytes 6144 | tf_op jit(solution)/shard_map/psum | solution.py:171
  479.9 2.5 collective-permute-start.17
  482.9 5.9 %collective-permute-done.17 = bf16[3,256]{1,0:T(4,128)(2,1)S(1)} collective-permute-done((bf16[3,256]{1,0:T(4,128)(2,1)S(1)}, bf16[3,256]{1,0:T(4,128)(2,1)S(1)}, u32[]{:S(2)}, u32[]{:S(2)}) %collective-permute-start.17) | collective-permute-done | bytes 1568 | tf_op jit(solution)/shard_map/ppermute | solution.py:18
  489.2 1.4 fusion.23
  490.6 5.6 %copy.79 = f32[1,3,7,256,256]{4,3,2,1,0:T(8,128)} copy(f32[1,3,7,256,256]{4,3,2,1,0:T(8,128)} %get-tuple-element.60) | data formatting | bytes 11010048
  496.3 0.9 copy.80
  (258 shorter events, 22.7 us)
Async XLA Ops:
  7.2 483.4 %all-reduce.3.cloned.1.call-start = ((), (), s32[]{:S(2)}) async-start(), calls=%async_computation | async-start | bytes 12582912 | tf_op jit(solution)/shard_map/psum | solution.py:171
  8.4 11.6 %collective-permute-start.1 = (bf16[3,256]{1,0:T(4,128)(2,1)S(1)}, bf16[3,256]{1,0:T(4,128)(2,1)S(1)}, u32[]{:S(2)}, u32[]{:S(2)}) collective-permute-start(bf16[3,256]{1,0:T(4,128)(2,1)S(1)} %get-tuple-element.28), channel_id=1, source_target_pairs={{2,0},{4,2},{6,4},{8,6},{10,8},{12,10},{14,12},{16,14},{18,16},{20... | collective-permute-start | bytes 4616 | tf_op jit(solution)/shard_map/ppermute | solution.py:20
  12.1 7.2 %collective-permute-start = (bf16[3,256]{1,0:T(4,128)(2,1)S(1)}, bf16[3,256]{1,0:T(4,128)(2,1)S(1)}, u32[]{:S(2)}, u32[]{:S(2)}) collective-permute-start(bf16[3,256]{1,0:T(4,128)(2,1)S(1)} %get-tuple-element.29), channel_id=1, source_target_pairs={{0,2},{2,4},{4,6},{6,8},{8,10},{10,12},{12,14},{14,16},{16,18},{18... | collective-permute-start | bytes 4616 | tf_op jit(solution)/shard_map/ppermute | solution.py:18
  15.4 12.7 %copy-start.30 = (pred[512]{0:T(512)(128)(4,1)}, pred[512]{0:T(512)(128)(4,1)S(1)}, u32[]{:S(2)}) copy-start(pred[512]{0:T(512)(128)(4,1)S(1)} %get-tuple-element.42) | copy-start | bytes 1540
  15.4 25.1 %copy-start.53 = (pred[512]{0:T(512)(128)(4,1)}, pred[512]{0:T(512)(128)(4,1)S(1)}, u32[]{:S(2)}) copy-start(pred[512]{0:T(512)(128)(4,1)S(1)} %get-tuple-element.43) | copy-start | bytes 1540
  15.4 30.0 %copy-start.56 = (pred[512]{0:T(512)(128)(4,1)}, pred[512]{0:T(512)(128)(4,1)S(1)}, u32[]{:S(2)}) copy-start(pred[512]{0:T(512)(128)(4,1)S(1)} %get-tuple-element.39) | copy-start | bytes 1540
  15.5 12.4 %copy-start.36 = (pred[512]{0:T(512)(128)(4,1)}, pred[512]{0:T(512)(128)(4,1)S(1)}, u32[]{:S(2)}) copy-start(pred[512]{0:T(512)(128)(4,1)S(1)} %get-tuple-element.34) | copy-start | bytes 1540
  15.5 16.9 %copy-start.23 = (pred[512]{0:T(512)(128)(4,1)}, pred[512]{0:T(512)(128)(4,1)S(1)}, u32[]{:S(2)}) copy-start(pred[512]{0:T(512)(128)(4,1)S(1)} %get-tuple-element.36) | copy-start | bytes 1540
  15.5 17.0 %copy-start.39 = (pred[512]{0:T(512)(128)(4,1)}, pred[512]{0:T(512)(128)(4,1)S(1)}, u32[]{:S(2)}) copy-start(pred[512]{0:T(512)(128)(4,1)S(1)} %get-tuple-element.33) | copy-start | bytes 1540
  15.5 25.1 %copy-start.42 = (pred[512]{0:T(512)(128)(4,1)}, pred[512]{0:T(512)(128)(4,1)S(1)}, u32[]{:S(2)}) copy-start(pred[512]{0:T(512)(128)(4,1)S(1)} %get-tuple-element.31) | copy-start | bytes 1540
  15.5 25.2 %copy-start.25 = (pred[512]{0:T(512)(128)(4,1)}, pred[512]{0:T(512)(128)(4,1)S(1)}, u32[]{:S(2)}) copy-start(pred[512]{0:T(512)(128)(4,1)S(1)} %get-tuple-element.35) | copy-start | bytes 1540
  15.6 29.7 %copy-start.28 = (pred[512]{0:T(512)(128)(4,1)}, pred[512]{0:T(512)(128)(4,1)S(1)}, u32[]{:S(2)}) copy-start(pred[512]{0:T(512)(128)(4,1)S(1)} %get-tuple-element.32) | copy-start | bytes 1540
  15.6 30.0 %copy-start.45 = (pred[512]{0:T(512)(128)(4,1)}, pred[512]{0:T(512)(128)(4,1)S(1)}, u32[]{:S(2)}) copy-start(pred[512]{0:T(512)(128)(4,1)S(1)} %get-tuple-element.30) | copy-start | bytes 1540
  21.9 12.2 %copy-start.12 = (f32[512,256]{1,0:T(8,128)}, f32[512,256]{1,0:T(8,128)S(1)}, u32[]{:S(2)}) copy-start(f32[512,256]{1,0:T(8,128)S(1)} %get-tuple-element.48) | copy-start | bytes 1572868
  21.9 5.9 %collective-permute-start.2 = (bf16[9,256]{1,0:T(8,128)(2,1)S(1)}, bf16[9,256]{1,0:T(8,128)(2,1)S(1)}, u32[]{:S(2)}, u32[]{:S(2)}) collective-permute-start(bf16[9,256]{1,0:T(8,128)(2,1)S(1)} %get-tuple-element.27), channel_id=1, source_target_pairs={{0,2},{2,4},{4,6},{6,8},{8,10},{10,12},{12,14},{14,16},{16,18},{18... | collective-permute-start | bytes 13832 | tf_op jit(solution)/shard_map/ppermute | solution.py:18
  25.8 6.7 %collective-permute-start.3 = (bf16[9,256]{1,0:T(8,128)(2,1)S(1)}, bf16[9,256]{1,0:T(8,128)(2,1)S(1)}, u32[]{:S(2)}, u32[]{:S(2)}) collective-permute-start(bf16[9,256]{1,0:T(8,128)(2,1)S(1)} %get-tuple-element.26), channel_id=1, source_target_pairs={{2,0},{4,2},{6,4},{8,6},{10,8},{12,10},{14,12},{16,14},{18,16},{20... | collective-permute-start | bytes 13832 | tf_op jit(solution)/shard_map/ppermute | solution.py:20
  34.5 24.3 %copy-start.18 = (f32[512,256]{1,0:T(8,128)}, f32[512,256]{1,0:T(8,128)S(1)}, u32[]{:S(2)}) copy-start(f32[512,256]{1,0:T(8,128)S(1)} %get-tuple-element.50) | copy-start | bytes 1572868
  34.6 5.9 %collective-permute-start.4 = (bf16[27,256]{1,0:T(8,128)(2,1)S(1)}, bf16[27,256]{1,0:T(8,128)(2,1)S(1)}, u32[]{:S(2)}, u32[]{:S(2)}) collective-permute-start(bf16[27,256]{1,0:T(8,128)(2,1)S(1)} %get-tuple-element.25), channel_id=1, source_target_pairs={{0,2},{2,4},{4,6},{6,8},{8,10},{10,12},{12,14},{14,16},{16,18},{18... | collective-permute-start | bytes 41480 | tf_op jit(solution)/shard_map/ppermute | solution.py:18
  38.5 6.7 %collective-permute-start.5 = (bf16[27,256]{1,0:T(8,128)(2,1)S(1)}, bf16[27,256]{1,0:T(8,128)(2,1)S(1)}, u32[]{:S(2)}, u32[]{:S(2)}) collective-permute-start(bf16[27,256]{1,0:T(8,128)(2,1)S(1)} %get-tuple-element.24), channel_id=1, source_target_pairs={{2,0},{4,2},{6,4},{8,6},{10,8},{12,10},{14,12},{16,14},{18,16},{20... | collective-permute-start | bytes 41480 | tf_op jit(solution)/shard_map/ppermute | solution.py:20
  47.8 8.2 %collective-permute-start.6 = (bf16[27,256]{1,0:T(8,128)(2,1)}, bf16[27,256]{1,0:T(8,128)(2,1)S(1)}, u32[]{:S(2)}, u32[]{:S(2)}) collective-permute-start(bf16[27,256]{1,0:T(8,128)(2,1)} %get-tuple-element.23), channel_id=1, source_target_pairs={{2,0},{4,2},{6,4},{8,6},{10,8},{12,10},{14,12},{16,14},{18,16},{20... | collective-permute-start | bytes 41480 | tf_op jit(solution)/shard_map/ppermute | solution.py:20
  52.0 6.4 %collective-permute-start.7 = (bf16[27,256]{1,0:T(8,128)(2,1)}, bf16[27,256]{1,0:T(8,128)(2,1)S(1)}, u32[]{:S(2)}, u32[]{:S(2)}) collective-permute-start(bf16[27,256]{1,0:T(8,128)(2,1)} %get-tuple-element.22), channel_id=1, source_target_pairs={{0,2},{2,4},{4,6},{6,8},{8,10},{10,12},{12,14},{14,16},{16,18},{18... | collective-permute-start | bytes 41480 | tf_op jit(solution)/shard_map/ppermute | solution.py:18
  60.0 9.6 %copy-start.29 = (pred[512]{0:T(512)(128)(4,1)S(1)}, pred[512]{0:T(512)(128)(4,1)}, u32[]{:S(2)}) copy-start(pred[512]{0:T(512)(128)(4,1)} %copy-done.28) | copy-start | bytes 1540
  60.0 9.7 %copy-start.40 = (pred[512]{0:T(512)(128)(4,1)S(1)}, pred[512]{0:T(512)(128)(4,1)}, u32[]{:S(2)}) copy-start(pred[512]{0:T(512)(128)(4,1)} %copy-done.39) | copy-start | bytes 1540
  60.0 9.9 %copy-start.24 = (pred[512]{0:T(512)(128)(4,1)S(1)}, pred[512]{0:T(512)(128)(4,1)}, u32[]{:S(2)}) copy-start(pred[512]{0:T(512)(128)(4,1)} %copy-done.23) | copy-start | bytes 1540
  61.3 8.3 %collective-permute-start.8 = (bf16[9,256]{1,0:T(8,128)(2,1)S(1)}, bf16[9,256]{1,0:T(8,128)(2,1)S(1)}, u32[]{:S(2)}, u32[]{:S(2)}) collective-permute-start(bf16[9,256]{1,0:T(8,128)(2,1)S(1)} %get-tuple-element.21), channel_id=1, source_target_pairs={{2,0},{4,2},{6,4},{8,6},{10,8},{12,10},{14,12},{16,14},{18,16},{20... | collective-permute-start | bytes 13832 | tf_op jit(solution)/shard_map/ppermute | solution.py:20
  63.2 7.9 %copy-start.31 = (pred[512]{0:T(512)(128)(4,1)S(1)}, pred[512]{0:T(512)(128)(4,1)}, u32[]{:S(2)}) copy-start(pred[512]{0:T(512)(128)(4,1)} %copy-done.30) | copy-start | bytes 1540
  63.2 8.1 %copy-start.37 = (pred[512]{0:T(512)(128)(4,1)S(1)}, pred[512]{0:T(512)(128)(4,1)}, u32[]{:S(2)}) copy-start(pred[512]{0:T(512)(128)(4,1)} %copy-done.36) | copy-start | bytes 1540
  65.5 5.7 %collective-permute-start.9 = (bf16[9,256]{1,0:T(8,128)(2,1)S(1)}, bf16[9,256]{1,0:T(8,128)(2,1)S(1)}, u32[]{:S(2)}, u32[]{:S(2)}) collective-permute-start(bf16[9,256]{1,0:T(8,128)(2,1)S(1)} %get-tuple-element.20), channel_id=1, source_target_pairs={{0,2},{2,4},{4,6},{6,8},{8,10},{10,12},{12,14},{14,16},{16,18},{18... | collective-permute-start | bytes 13832 | tf_op jit(solution)/shard_map/ppermute | solution.py:18
  74.6 7.7 %collective-permute-start.10 = (bf16[3,256]{1,0:T(4,128)(2,1)}, bf16[3,256]{1,0:T(4,128)(2,1)}, u32[]{:S(2)}, u32[]{:S(2)}) collective-permute-start(bf16[3,256]{1,0:T(4,128)(2,1)} %get-tuple-element.19), channel_id=1, source_target_pairs={{2,0},{4,2},{6,4},{8,6},{10,8},{12,10},{14,12},{16,14},{18,16},{20... | collective-permute-start | bytes 4616 | tf_op jit(solution)/shard_map/ppermute | solution.py:20
  77.9 7.3 %copy-start.72 = (bf16[512,256]{1,0:T(8,128)(2,1)S(1)}, bf16[512,256]{1,0:T(8,128)(2,1)}, u32[]{:S(2)}) copy-start(bf16[512,256]{1,0:T(8,128)(2,1)} %copy-done.71) | copy-start | bytes 786436
  77.9 6.9 %collective-permute-start.11 = (bf16[3,256]{1,0:T(4,128)(2,1)}, bf16[3,256]{1,0:T(4,128)(2,1)S(1)}, u32[]{:S(2)}, u32[]{:S(2)}) collective-permute-start(bf16[3,256]{1,0:T(4,128)(2,1)} %get-tuple-element.18), channel_id=1, source_target_pairs={{0,2},{2,4},{4,6},{6,8},{8,10},{10,12},{12,14},{14,16},{16,18},{18... | collective-permute-start | bytes 4616 | tf_op jit(solution)/shard_map/ppermute | solution.py:18
  91.7 10.0 %copy-start.46 = (pred[512]{0:T(512)(128)(4,1)S(1)}, pred[512]{0:T(512)(128)(4,1)}, u32[]{:S(2)}) copy-start(pred[512]{0:T(512)(128)(4,1)} %copy-done.45) | copy-start | bytes 1540
  94.0 7.9 %copy-start.57 = (pred[512]{0:T(512)(128)(4,1)S(1)}, pred[512]{0:T(512)(128)(4,1)}, u32[]{:S(2)}) copy-start(pred[512]{0:T(512)(128)(4,1)} %copy-done.56) | copy-start | bytes 1540
  94.0 9.3 %copy-start.44 = (pred[512]{0:T(512)(128)(4,1)S(1)}, pred[512]{0:T(512)(128)(4,1)}, u32[]{:S(2)}) copy-start(pred[512]{0:T(512)(128)(4,1)} %copy-done.42) | copy-start | bytes 1540
  94.0 7.7 %collective-permute-start.12 = (bf16[27,256]{1,0:T(8,128)(2,1)S(1)}, bf16[27,256]{1,0:T(8,128)(2,1)S(1)}, u32[]{:S(2)}, u32[]{:S(2)}) collective-permute-start(bf16[27,256]{1,0:T(8,128)(2,1)S(1)} %get-tuple-element.17), channel_id=1, source_target_pairs={{2,0},{4,2},{6,4},{8,6},{10,8},{12,10},{14,12},{16,14},{18,16},{20... | collective-permute-start | bytes 41480 | tf_op jit(solution)/shard_map/ppermute | solution.py:20
  96.4 6.7 %collective-permute-start.13 = (bf16[27,256]{1,0:T(8,128)(2,1)S(1)}, bf16[27,256]{1,0:T(8,128)(2,1)S(1)}, u32[]{:S(2)}, u32[]{:S(2)}) collective-permute-start(bf16[27,256]{1,0:T(8,128)(2,1)S(1)} %get-tuple-element.16), channel_id=1, source_target_pairs={{0,2},{2,4},{4,6},{6,8},{8,10},{10,12},{12,14},{14,16},{16,18},{18... | collective-permute-start | bytes 41480 | tf_op jit(solution)/shard_map/ppermute | solution.py:18
  106.1 8.1 %copy-start.41 = (pred[512]{0:T(512)(128)(4,1)S(1)}, pred[512]{0:T(512)(128)(4,1)}, u32[]{:S(2)}) copy-start(pred[512]{0:T(512)(128)(4,1)} %copy-done.39) | copy-start | bytes 1540
  106.1 9.4 %copy-start.38 = (pred[512]{0:T(512)(128)(4,1)S(1)}, pred[512]{0:T(512)(128)(4,1)}, u32[]{:S(2)}) copy-start(pred[512]{0:T(512)(128)(4,1)} %copy-done.36) | copy-start | bytes 1540
  106.1 7.9 %collective-permute-start.14 = (bf16[9,256]{1,0:T(8,128)(2,1)S(1)}, bf16[9,256]{1,0:T(8,128)(2,1)S(1)}, u32[]{:S(2)}, u32[]{:S(2)}) collective-permute-start(bf16[9,256]{1,0:T(8,128)(2,1)S(1)} %get-tuple-element.15), channel_id=1, source_target_pairs={{2,0},{4,2},{6,4},{8,6},{10,8},{12,10},{14,12},{16,14},{18,16},{20... | collective-permute-start | bytes 13832 | tf_op jit(solution)/shard_map/ppermute | solution.py:20
  108.5 6.9 %collective-permute-start.15 = (bf16[9,256]{1,0:T(8,128)(2,1)S(1)}, bf16[9,256]{1,0:T(8,128)(2,1)S(1)}, u32[]{:S(2)}, u32[]{:S(2)}) collective-permute-start(bf16[9,256]{1,0:T(8,128)(2,1)S(1)} %get-tuple-element.14), channel_id=1, source_target_pairs={{0,2},{2,4},{4,6},{6,8},{8,10},{10,12},{12,14},{14,16},{16,18},{18... | collective-permute-start | bytes 13832 | tf_op jit(solution)/shard_map/ppermute | solution.py:18
  122.1 360.4 %copy-start.35 = (pred[512]{0:T(512)(128)(4,1)S(1)}, pred[512]{0:T(512)(128)(4,1)}, u32[]{:S(2)}) copy-start(pred[512]{0:T(512)(128)(4,1)} %copy-done.34) | copy-start | bytes 1540
  122.1 360.6 %copy-start.33 = (pred[512]{0:T(512)(128)(4,1)S(1)}, pred[512]{0:T(512)(128)(4,1)}, u32[]{:S(2)}) copy-start(pred[512]{0:T(512)(128)(4,1)} %copy-done.32) | copy-start | bytes 1540
  122.1 366.6 %copy-start.52 = (pred[512]{0:T(512)(128)(4,1)S(1)}, pred[512]{0:T(512)(128)(4,1)}, u32[]{:S(2)}) copy-start(pred[512]{0:T(512)(128)(4,1)} %copy-done.50) | copy-start | bytes 1540
  122.1 366.7 %copy-start.49 = (pred[512]{0:T(512)(128)(4,1)S(1)}, pred[512]{0:T(512)(128)(4,1)}, u32[]{:S(2)}) copy-start(pred[512]{0:T(512)(128)(4,1)} %copy-done.47) | copy-start | bytes 1540
  122.8 359.6 %collective-permute-start.16 = (bf16[3,256]{1,0:T(4,128)(2,1)S(1)}, bf16[3,256]{1,0:T(4,128)(2,1)S(1)}, u32[]{:S(2)}, u32[]{:S(2)}) collective-permute-start(bf16[3,256]{1,0:T(4,128)(2,1)S(1)} %get-tuple-element.13), channel_id=1, source_target_pairs={{2,0},{4,2},{6,4},{8,6},{10,8},{12,10},{14,12},{16,14},{18,16},{20... | collective-permute-start | bytes 4616 | tf_op jit(solution)/shard_map/ppermute | solution.py:20
  479.9 9.3 %copy-start.6 = (bf16[7,256,256]{2,1,0:T(8,128)(2,1)S(1)}, bf16[7,256,256]{2,1,0:T(8,128)(2,1)}, u32[]{:S(2)}) copy-start(bf16[7,256,256]{2,1,0:T(8,128)(2,1)} %copy.22) | copy-start | bytes 2752516
  479.9 9.3 %copy-start.74 = (bf16[512,256]{1,0:T(8,128)(2,1)S(1)}, bf16[512,256]{1,0:T(8,128)(2,1)}, u32[]{:S(2)}) copy-start(bf16[512,256]{1,0:T(8,128)(2,1)} %get-tuple-element.52) | copy-start | bytes 786436
  479.9 8.8 %collective-permute-start.17 = (bf16[3,256]{1,0:T(4,128)(2,1)S(1)}, bf16[3,256]{1,0:T(4,128)(2,1)S(1)}, u32[]{:S(2)}, u32[]{:S(2)}) collective-permute-start(bf16[3,256]{1,0:T(4,128)(2,1)S(1)} %get-tuple-element.12), channel_id=1, source_target_pairs={{0,2},{2,4},{4,6},{6,8},{8,10},{10,12},{12,14},{14,16},{16,18},{18... | collective-permute-start | bytes 4616 | tf_op jit(solution)/shard_map/ppermute | solution.py:18
  (46 other events, 201.4 us)
Sparse Core Ops, SparseCore 0:
  122.3 255.6 all-reduce.2
